TPU v7x, 256 devices: a whole 4x4x8 slice. The times are simulated.
256 devices in a mesh: seq: 8 (over z), exp: 8 (over x, y_hi), img: 4 (over y_lo, core).
Axes of the slice: x: 4, y: 4 (y_hi: 2, y_lo: 2; y = y_hi * 2 + y_lo), z: 8, core: 2. Of those that a mesh axis runs over, the one named last changes fastest.
Arguments:
- projected: bfloat16 [32, 1024, 3, 1280], P(('img', 'exp'), 'seq'), parts along dimension 0, may hold values from -6 to 6
- residual: bfloat16 [32, 1024, 1280], P(('img', 'exp'), 'seq'), parts along dimension 0, may hold values from -6 to 6
- attn_proj: bfloat16 [1280, 1280], P('seq'), may hold values from -0.15625 to 0.15625
- norm_gain: float32 [1280], replicated, may hold values from 0.5 to 2
- norm_bias: float32 [1280], replicated, may hold values from -3 to 3
- expert_ids: int32 [32, 1024, 1], P(('img', 'exp')), parts along dimension 0, may hold values from 0 to 15; in each aligned block of 128 rows (0 to 127, 128 to 255, ..., all dimensions but the last counted through in order) at most 12 rows name the same one
- expert_up: bfloat16 [16, 1280, 5120], P('exp', None, 'seq'), may hold values from -0.15625 to 0.15625
- expert_down: bfloat16 [16, 5120, 1280], P('exp', 'seq'), may hold values from -0.078125 to 0.078125
Outputs:
- layer_out: bfloat16 [32, 1024, 1280], P(('img', 'exp'), 'seq'), parts along dimension 0
There are 4 independent parts, one for each index of `img`. A program takes and returns all parts, laid end to end along the dimension named above; an argument that names none is the same for every part. Nothing has to cross between parts.
Inputs may be any that keep to these rules, and one draw needn't show every extreme that they name: `expert_ids`: in each sequence, within every aligned block of 128 tokens, no expert is named by more than 12 tokens.
All inputs are finite; a program needn't handle non-finite values.
Results may differ from a plain program's by a relative error of at most 0.015.
Values may be sent and summed in bfloat16 or wider, within the bound.
No kernel may reach another device: no remote copies, remote signals or barrier semaphores. Data moves between devices by JAX's collectives and lax.ppermute only.
A program may use at most 64 MiB of HBM per device.

v0:
```python
import jax
import jax.numpy as jnp
from jax import lax
from jax.sharding import PartitionSpec as P

HEADS = 16
HEAD_DIM = 80


def attend(gathered):
    queries = gathered[0]
    keys_all = gathered[1]
    values = gathered[2]
    factor = 1.0 / queries.shape[2] ** 0.5
    scores = (
        jnp.einsum("ahdb,chde->habce", queries, keys_all, preferred_element_type=jnp.float32)
        * factor
    )
    peak = jnp.max(scores, axis=(3, 4), keepdims=True)
    powers = jnp.exp(scores - peak)
    weights = (powers * (1.0 / jnp.sum(powers, axis=(3, 4), keepdims=True))).astype(jnp.bfloat16)
    mixed = jnp.einsum("habce,chde->abhd", weights, values, preferred_element_type=jnp.float32)
    return mixed.astype(jnp.bfloat16)


def layer_norm(stream, norm_gain, norm_bias):
    values = stream.astype(jnp.float32)
    centre = jnp.mean(values, axis=-1, keepdims=True)
    centered = values - centre
    variance = jnp.mean(centered * centered, axis=-1, keepdims=True)
    return (centered * lax.rsqrt(variance + 1e-06) * norm_gain + norm_bias).astype(jnp.bfloat16)


def per_device(
    projected, residual, attn_proj, norm_gain, norm_bias, expert_ids, expert_up, expert_down
):
    tok_rows = projected.shape[1]
    model_width = projected.shape[3]
    seq_count = lax.axis_size("seq")
    exp_count = lax.axis_size("exp")
    local_experts = expert_up.shape[0]
    experts = local_experts * exp_count
    cap_dev = 3 * tok_rows // (2 * experts)
    capacity = cap_dev * seq_count
    length = tok_rows * seq_count
    heads_here = HEADS // seq_count
    head_width = heads_here * HEAD_DIM
    token_minor = jnp.transpose(projected[0], (1, 2, 0)).reshape(3, seq_count, head_width, tok_rows)
    arrived_heads = lax.all_to_all(token_minor, "seq", split_axis=1, concat_axis=1, tiled=True)
    attended = attend(arrived_heads.reshape(3, seq_count, heads_here, HEAD_DIM, tok_rows))
    attended = attended.reshape(seq_count, tok_rows, 1, head_width)
    token_heads = lax.all_to_all(attended, "seq", split_axis=0, concat_axis=2, tiled=True).reshape(
        tok_rows, model_width
    )
    projected_sum = jnp.dot(
        token_heads,
        lax.all_gather(attn_proj, "seq", axis=0, tiled=True),
        preferred_element_type=jnp.float32,
    )
    stream_own = residual[0].astype(jnp.float32) + projected_sum
    stream = stream_own.astype(jnp.bfloat16)
    stream_own = stream.astype(jnp.float32)
    normed = layer_norm(stream, norm_gain, norm_bias)
    seq_index = lax.axis_index("seq")
    ids_own = lax.dynamic_slice_in_dim(expert_ids[0, :, 0], seq_index * tok_rows, tok_rows)
    onehot = (ids_own[:, None] == jnp.arange(experts, dtype=jnp.int32)[None, :]).astype(jnp.int32)
    before = jnp.cumsum(onehot, axis=0) - onehot
    order_in_block = jnp.sum(before * onehot, axis=1)
    dest = ids_own * cap_dev + order_in_block
    select = (
        (dest[:, None] == jnp.arange(experts * cap_dev, dtype=jnp.int32)[None, :])
        .astype(jnp.bfloat16)
        .reshape(tok_rows, exp_count, local_experts, cap_dev)
    )
    dispatch = jnp.einsum(
        "tgjc,td->gjcd", select, normed, preferred_element_type=jnp.float32
    ).astype(jnp.bfloat16)
    arrived = lax.all_to_all(dispatch, "exp", split_axis=0, concat_axis=0, tiled=True)
    gathered = lax.all_gather(arrived, "seq", axis=0, tiled=False)
    pieces = []
    for local in range(local_experts):
        lifted = jnp.einsum(
            "secd,df->secf",
            gathered[:, :, local],
            expert_up[local],
            preferred_element_type=jnp.float32,
        )
        hidden = (0.5 * lifted * (1.0 + lax.erf(lifted * 0.5**0.5))).astype(jnp.bfloat16)
        hidden = lax.optimization_barrier(hidden)
        piece = jnp.einsum(
            "secf,fd->secd", hidden, expert_down[local], preferred_element_type=jnp.float32
        )
        pieces.append(piece.astype(jnp.bfloat16))
    pieces = jnp.stack(pieces, axis=2)
    summed = lax.psum_scatter(pieces, "seq", scatter_dimension=0, tiled=True)[0]
    returned = lax.all_to_all(summed, "exp", split_axis=0, concat_axis=0, tiled=True)
    expert_out = jnp.einsum("tgjc,gjcd->td", select, returned, preferred_element_type=jnp.float32)
    return (stream_own + expert_out).astype(jnp.bfloat16)[None]


def solution(mesh):
    return jax.shard_map(
        per_device,
        mesh=mesh,
        in_specs=(
            P(("img", "exp"), "seq", None, None),
            P(("img", "exp"), "seq", None),
            P("seq", None),
            P(),
            P(),
            P(("img", "exp"), None, None),
            P("exp", None, "seq"),
            P("exp", "seq", None),
        ),
        out_specs=P(("img", "exp"), "seq", None),
        check_vma=False,
    )
```

profile of v0, /device:TPU:8, one launch (start us, length us, event | category | flops | bytes accessed | tf_op | source)
XLA Modules:
  0.0 244.4 jit_solution(5946868216613501484)
XLA Ops:
  7.3 1.6 copy.22
  8.9 1.0 copy.23
  9.9 8.5 %all-to-all-start = ((bf16[3,8,160,128]{3,2,0,1:T(8,128)(2,1)}), bf16[3,8,160,128]{3,2,0,1:T(8,128)(2,1)S(1)}, u32[]{:S(2)}, u32[]{:S(2)}) async-start(bf16[3,8,160,128]{3,2,0,1:T(8,128)(2,1)} %copy.23), calls=%async_computation | async-start | bytes 1966080 | tf_op jit(solution)/shard_map/all_to_all | solution.py:49
  19.0 36.1 %all-to-all-done = bf16[3,8,160,128]{3,2,0,1:T(8,128)(2,1)S(1)} async-done(((bf16[3,8,160,128]{3,2,0,1:T(8,128)(2,1)}), bf16[3,8,160,128]{3,2,0,1:T(8,128)(2,1)S(1)}, u32[]{:S(2)}, u32[]{:S(2)}) %all-to-all-start) | async-done | bytes 983072 | tf_op jit(solution)/shard_map/all_to_all | solution.py:49
  55.2 1.3 multiply_reduce_fusion
  56.5 1.4 fusion
  57.9 1.8 fusion.25
  59.7 0.7 copy.31
  60.5 3.4 %all-to-all-start.1 = ((bf16[8,128,1,160]{1,3,2,0:T(8,128)(2,1)}), bf16[8,128,1,160]{1,3,2,0:T(8,128)(2,1)S(1)}, u32[]{:S(2)}, u32[]{:S(2)}) async-start(bf16[8,128,1,160]{1,3,2,0:T(8,128)(2,1)} %bitcast.13), calls=%async_computation.1 | async-start | bytes 655360 | tf_op jit(solution)/shard_map/all_to_all | solution.py:52
  65.1 16.4 %all-to-all-done.1 = bf16[8,128,1,160]{1,3,2,0:T(8,128)(2,1)S(1)} async-done(((bf16[8,128,1,160]{1,3,2,0:T(8,128)(2,1)}), bf16[8,128,1,160]{1,3,2,0:T(8,128)(2,1)S(1)}, u32[]{:S(2)}, u32[]{:S(2)}) %all-to-all-start.1) | async-done | bytes 327712 | tf_op jit(solution)/shard_map/all_to_all | solution.py:52
  81.5 2.6 %fusion.46 = (f32[128]{0:T(128)S(1)}, f32[128,1280]{1,0:T(8,128)S(1)}) fusion(bf16[128,1280]{0,1:T(8,128)(2,1)S(1)} %bitcast.114, bf16[1280,1280]{1,0:T(8,128)(2,1)} %all-gather.4.cloned.1.call-done, bf16[1,128,1280]{2,1,0:T(8,128)(2,1)S(1)} %copy-done), kind=kOutput, calls=%fused_computation.64 | convolution fusion | flops 420249472 | bytes 4588032 | tf_op jit(solution)/shard_map/dot_general | solution.py:55
  85.2 16.5 %all_to_all.30 = bf16[8,2,12,1280]{3,1,2,0:T(2,128)(2,1)} all-to-all(bf16[8,2,12,1280]{3,1,2,0:T(2,128)(2,1)S(1)} %copy.32), channel_id=1, replica_groups=mesh['seq'=8,'exp'=8,'img'=4] {'exp'}, dimensions={0} | all-to-all | bytes 983040 | tf_op jit(solution)/shard_map/all_to_all | solution.py:78
  101.9 48.6 %all-gather.6.cloned.1.call-done = bf16[64,2,12,1280]{3,1,2,0:T(2,128)(2,1)} async-done(((bf16[8,2,12,1280]{3,1,2,0:T(2,128)(2,1)}), bf16[64,2,12,1280]{3,1,2,0:T(2,128)(2,1)}) %all-gather.6.cloned.1.call-update) | async-done | bytes 3932176 | tf_op jit(solution)/shard_map/all_gather | solution.py:79
  150.5 3.0 %copy.33 = bf16[64,2,12,1280]{3,2,0,1:T(8,128)(2,1)S(1)} copy(bf16[64,2,12,1280]{3,1,2,0:T(2,128)(2,1)} %all-gather.6.cloned.1.call-done) | data formatting | bytes 7864320 | tf_op jit(solution)/shard_map/all_gather | solution.py:79
  153.6 2.4 multiply_convert_fusion.3
  156.1 2.4 multiply_convert_fusion.2
  158.5 2.2 fusion.2
  160.8 2.2 fusion.3
  163.0 0.7 pad_maximum_fusion
  163.7 3.4 %copy.34 = bf16[8,8,2,12,1280]{4,1,3,2,0:T(8,128)(2,1)} copy(bf16[8,8,2,12,1280]{4,3,1,0,2:T(8,128)(2,1)S(1)} %pad_maximum_fusion) | data formatting | bytes 7864320 | tf_op jit(solution)/shard_map/stack | solution.py:94
  167.1 51.6 %reduce-scatter.2.cloned.1.call-done = bf16[1,8,2,12,1280]{4,1,3,2,0:T(8,128)(2,1)} async-done(((bf16[8,8,2,12,1280]{4,1,3,2,0:T(8,128)(2,1)}), bf16[1,8,2,12,1280]{4,1,3,2,0:T(8,128)(2,1)}) %reduce-scatter.2.cloned.1.call-update) | async-done | bytes 491536 | tf_op jit(solution)/shard_map/reduce_scatter | solution.py:95
  218.7 1.5 copy.35
  220.2 16.5 %all_to_all.31 = bf16[8,2,12,1280]{3,1,2,0:T(2,128)(2,1)S(1)} all-to-all(bf16[8,2,12,1280]{3,1,2,0:T(2,128)(2,1)S(1)} %copy.35), channel_id=1, replica_groups=mesh['seq'=8,'exp'=8,'img'=4] {'exp'}, dimensions={0} | all-to-all | bytes 983040 | tf_op jit(solution)/shard_map/all_to_all | solution.py:96
  236.7 1.1 fusion.10
  (30 shorter events, 4.0 us)
Async XLA Ops:
  6.5 74.9 %all-gather.4.cloned.1.call-start = ((), (), s32[]{:S(2)}) async-start(), calls=%async_computation.5 | async-start | bytes 3686400 | tf_op jit(solution)/shard_map/all_gather | solution.py:57
  9.9 45.2 %all-to-all-start = ((bf16[3,8,160,128]{3,2,0,1:T(8,128)(2,1)}), bf16[3,8,160,128]{3,2,0,1:T(8,128)(2,1)S(1)}, u32[]{:S(2)}, u32[]{:S(2)}) async-start(bf16[3,8,160,128]{3,2,0,1:T(8,128)(2,1)} %copy.23), calls=%async_computation | async-start | bytes 1966080 | tf_op jit(solution)/shard_map/all_to_all | solution.py:49
  57.9 23.6 %copy-start = (bf16[1,128,1280]{2,1,0:T(8,128)(2,1)S(1)}, bf16[1,128,1280]{2,1,0:T(8,128)(2,1)}, u32[]{:S(2)}) copy-start(bf16[1,128,1280]{2,1,0:T(8,128)(2,1)} %param.9) | copy-start | bytes 983044
  59.7 24.7 %copy-start.1 = (f32[1280]{0:T(1024)S(1)}, f32[1280]{0:T(1024)}, u32[]{:S(2)}) copy-start(f32[1280]{0:T(1024)} %param.12) | copy-start | bytes 15364
  59.7 24.7 %copy-start.2 = (f32[1280]{0:T(1024)S(1)}, f32[1280]{0:T(1024)}, u32[]{:S(2)}) copy-start(f32[1280]{0:T(1024)} %param.11) | copy-start | bytes 15364
  60.5 21.0 %all-to-all-start.1 = ((bf16[8,128,1,160]{1,3,2,0:T(8,128)(2,1)}), bf16[8,128,1,160]{1,3,2,0:T(8,128)(2,1)S(1)}, u32[]{:S(2)}, u32[]{:S(2)}) async-start(bf16[8,128,1,160]{1,3,2,0:T(8,128)(2,1)} %bitcast.13), calls=%async_computation.1 | async-start | bytes 655360 | tf_op jit(solution)/shard_map/all_to_all | solution.py:52
  63.9 86.6 %all-gather.6.cloned.1.call-start = ((), (), s32[]{:S(2)}) async-start(), calls=%async_computation.7 | async-start | bytes 4423680 | tf_op jit(solution)/shard_map/all_gather | solution.py:79
  101.7 117.0 %reduce-scatter.2.cloned.1.call-start = ((), (), s32[]{:S(2)}) async-start(), calls=%async_computation.6 | async-start | bytes 4423680 | tf_op jit(solution)/shard_map/reduce_scatter | solution.py:95
  150.5 3.1 %copy-start.3 = (bf16[2,1280,640]{2,1,0:T(8,128)(2,1)S(1)}, bf16[2,1280,640]{2,1,0:T(8,128)(2,1)}, u32[]{:S(2)}) copy-start(bf16[2,1280,640]{2,1,0:T(8,128)(2,1)} %param.14) | copy-start | bytes 9830404
  156.1 2.5 %copy-start.4 = (bf16[2,640,1280]{2,1,0:T(8,128)(2,1)S(1)}, bf16[2,640,1280]{2,1,0:T(8,128)(2,1)}, u32[]{:S(2)}) copy-start(bf16[2,640,1280]{2,1,0:T(8,128)(2,1)} %param.15) | copy-start | bytes 9830404
Sparse Core Ops, SparseCore 0:
  9.1 71.9 all-gather.3
  101.8 48.6 all-gather.5
  167.2 51.4 reduce-scatter.1
where the time goes:
time: 245 us; the launch traced here: 244 us
  waiting for transfers between devices  153 us (62%)
  blocking collectives  32.9 us (13%)
  matrix products  16.6 us (7%)
  between operations  13.3 us (5%)
  local copies, waits for them, and re-layouts  12.5 us (5%)
  starting transfers between devices  12.2 us (5%)
  other arithmetic  3.42 us (1%)
    reduce_scatter x1, waiting for transfers between devices, per_device(): summed = lax.psum_scatter(pieces, 'seq', scatter_dimension=0, tiled=True)[0]  51.6 us
    all_gather x1, waiting for transfers between devices, per_device(): gathered = lax.all_gather(arrived, 'seq', axis=0, tiled=False)  48.6 us
    all_to_all x1, waiting for transfers between devices, per_device(): lax.all_to_all(token_minor, 'seq', split_axis=1, concat_axis=1, tiled=True)  36.1 us
    all_to_all x1, blocking collectives, per_device(): lax.all_to_all(summed, 'exp', split_axis=0, concat_axis=0, tiled=True)  16.5 us
    all_to_all x1, blocking collectives, per_device(): lax.all_to_all(dispatch, 'exp', split_axis=0, concat_axis=0, tiled=True)  16.5 us
    all_to_all x1, waiting for transfers between devices, per_device(): lax.all_to_all(attended, 'seq', split_axis=0, concat_axis=2, tiled=True)  16.4 us
    all_to_all x1, starting transfers between devices, per_device(): lax.all_to_all(token_minor, 'seq', split_axis=1, concat_axis=1, tiled=True)  8.47 us
  transfers between devices with their start and end apart: 5, of which 4 were waited for; matrix products, arithmetic and copies ran while one was open for 4% of the time, Pallas kernels for 0%

commit v1 on v0

--- a/solution.py
+++ b/solution.py
@@ -49,9 +49,10 @@
     arrived_heads = lax.all_to_all(token_minor, "seq", split_axis=1, concat_axis=1, tiled=True)
     attended = attend(arrived_heads.reshape(3, seq_count, heads_here, HEAD_DIM, tok_rows))
     attended = attended.reshape(seq_count, tok_rows, 1, head_width)
-    token_heads = lax.all_to_all(attended, "seq", split_axis=0, concat_axis=2, tiled=True).reshape(
-        tok_rows, model_width
-    )
+    token_heads = jnp.concatenate(
+        lax.all_to_all(jnp.stack(jnp.split(attended, lax.axis_size("seq"), axis=0)), "seq", 0, 0),
+        axis=2,
+    ).reshape(tok_rows, model_width)
     projected_sum = jnp.dot(
         token_heads,
         lax.all_gather(attn_proj, "seq", axis=0, tiled=True),

time: 245 us -> 244 us (level)
  waiting for transfers between devices: 153 us -> 148 us
  local copies, waits for them, and re-layouts: 12.5 us -> 16.8 us
    unnamed x11 -> x18, local copies, waits for them, and re-layouts: 1.72 us -> 6.06 us
    all_gather x1, waiting for transfers between devices: 48.6 us -> 45.5 us  [per_device(): gathered = lax.all_gather(arrived, 'seq', axis=0, tiled=False)]
  transfers between devices with their start and end apart: 5 -> 5, of which waited for: 4 -> 4; matrix products, arithmetic and copies ran while one was open for 4% -> 6% of each run, Pallas kernels for 0% -> 0%
where the time goes in v1:
time: 244 us
  waiting for transfers between devices  148 us (61%)
  blocking collectives  33.4 us (14%)
  local copies, waits for them, and re-layouts  16.8 us (7%)
  matrix products  16.6 us (7%)
  between operations  13.3 us (5%)
  starting transfers between devices  12.2 us (5%)
  other arithmetic  3.42 us (1%)
    reduce_scatter x1, waiting for transfers between devices, per_device(): summed = lax.psum_scatter(pieces, 'seq', scatter_dimension=0, tiled=True)[0]  51.6 us
    all_gather x1, waiting for transfers between devices, per_device(): gathered = lax.all_gather(arrived, 'seq', axis=0, tiled=False)  45.5 us
    all_to_all x1, waiting for transfers between devices, per_device(): lax.all_to_all(token_minor, 'seq', split_axis=1, concat_axis=1, tiled=True)  36.1 us
    all_to_all x1, blocking collectives, per_device(): lax.all_to_all(dispatch, 'exp', split_axis=0, concat_axis=0, tiled=True)  16.9 us
    all_to_all x1, blocking collectives, per_device(): lax.all_to_all(summed, 'exp', split_axis=0, concat_axis=0, tiled=True)  16.5 us
    all_to_all x1, waiting for transfers between devices, per_device(): lax.all_to_all(jnp.stack(jnp.split(attended, lax.axis_size('seq'), axis=0...  14.1 us
    all_to_all x1, starting transfers between devices, per_device(): lax.all_to_all(token_minor, 'seq', split_axis=1, concat_axis=1, tiled=True)  8.47 us
    unnamed x18, local copies, waits for them, and re-layouts  6.06 us
  transfers between devices with their start and end apart: 5, of which 4 were waited for; matrix products, arithmetic and copies ran while one was open for 6% of the time, Pallas kernels for 0%

profile of v1, /device:TPU:8, one launch (start us, length us, event | category | flops | bytes accessed | tf_op | source)
XLA Modules:
  0.0 243.6 jit_solution(9458520055724460635)
XLA Ops:
  6.5 0.7 all-gather.4.cloned.1.call-update
  7.3 1.6 copy.21
  8.9 1.0 copy.22
  9.9 8.5 %all-to-all-start = ((bf16[3,8,160,128]{3,2,0,1:T(8,128)(2,1)}), bf16[3,8,160,128]{3,2,0,1:T(8,128)(2,1)S(1)}, u32[]{:S(2)}, u32[]{:S(2)}) async-start(bf16[3,8,160,128]{3,2,0,1:T(8,128)(2,1)} %copy.22), calls=%async_computation | async-start | bytes 1966080 | tf_op jit(solution)/shard_map/all_to_all | solution.py:49
  19.0 36.1 %all-to-all-done = bf16[3,8,160,128]{3,2,0,1:T(8,128)(2,1)S(1)} async-done(((bf16[3,8,160,128]{3,2,0,1:T(8,128)(2,1)}), bf16[3,8,160,128]{3,2,0,1:T(8,128)(2,1)S(1)}, u32[]{:S(2)}, u32[]{:S(2)}) %all-to-all-start) | async-done | bytes 983072 | tf_op jit(solution)/shard_map/all_to_all | solution.py:49
  55.1 1.3 multiply_reduce_fusion
  56.5 1.4 fusion
  57.9 1.8 fusion.25
  64.7 3.4 %all-to-all-start.1 = ((bf16[8,1,128,1,160]{2,4,3,1,0:T(8,128)(2,1)}), bf16[8,1,128,1,160]{2,4,3,1,0:T(8,128)(2,1)S(1)}, u32[]{:S(2)}, u32[]{:S(2)}) async-start(bf16[8,1,128,1,160]{2,4,3,1,0:T(8,128)(2,1)} %constant_dynamic-update-slice_fusion), calls=%async_computation.1 | async-start | bytes 655360 | tf_op jit(solution)/shard_map/all_to_all | solution.py:53
  69.3 14.1 %all-to-all-done.1 = bf16[8,1,128,1,160]{2,4,3,1,0:T(8,128)(2,1)S(1)} async-done(((bf16[8,1,128,1,160]{2,4,3,1,0:T(8,128)(2,1)}), bf16[8,1,128,1,160]{2,4,3,1,0:T(8,128)(2,1)S(1)}, u32[]{:S(2)}, u32[]{:S(2)}) %all-to-all-start.1) | async-done | bytes 327712 | tf_op jit(solution)/shard_map/all_to_all | solution.py:53
  83.4 2.6 %fusion.47 = (f32[128]{0:T(128)S(1)}, f32[128,1280]{1,0:T(8,128)S(1)}) fusion(bf16[128,1280]{0,1:T(8,128)(2,1)S(1)} %bitcast.119, bf16[1280,1280]{1,0:T(8,128)(2,1)} %all-gather.4.cloned.1.call-done, bf16[1,128,1280]{2,1,0:T(8,128)(2,1)S(1)} %copy-done), kind=kOutput, calls=%fused_computation.73 | convolution fusion | flops 420249472 | bytes 4588032 | tf_op jit(solution)/shard_map/dot_general | solution.py:56
  87.2 16.9 %all_to_all.20 = bf16[8,2,12,1280]{3,1,2,0:T(2,128)(2,1)} all-to-all(bf16[8,2,12,1280]{3,1,2,0:T(2,128)(2,1)S(1)} %copy.30), channel_id=1, replica_groups=mesh['seq'=8,'exp'=8,'img'=4] {'exp'}, dimensions={0} | all-to-all | bytes 983040 | tf_op jit(solution)/shard_map/all_to_all | solution.py:79
  104.3 45.5 %all-gather.6.cloned.1.call-done = bf16[64,2,12,1280]{3,1,2,0:T(2,128)(2,1)} async-done(((bf16[8,2,12,1280]{3,1,2,0:T(2,128)(2,1)}), bf16[64,2,12,1280]{3,1,2,0:T(2,128)(2,1)}) %all-gather.6.cloned.1.call-update) | async-done | bytes 3932176 | tf_op jit(solution)/shard_map/all_gather | solution.py:80
  149.8 3.0 %copy.31 = bf16[64,2,12,1280]{3,2,0,1:T(8,128)(2,1)S(1)} copy(bf16[64,2,12,1280]{3,1,2,0:T(2,128)(2,1)} %all-gather.6.cloned.1.call-done) | data formatting | bytes 7864320 | tf_op jit(solution)/shard_map/all_gather | solution.py:80
  152.9 2.4 multiply_convert_fusion.3
  155.4 2.4 %multiply_convert_fusion.2 = bf16[8,8,12,640]{3,2,1,0:T(8,128)(2,1)S(1)} fusion(bf16[2,1280,640]{2,1,0:T(8,128)(2,1)S(1)} %copy-done.3, bf16[8,8,2,12,1280]{4,3,1,0,2:T(8,128)(2,1)S(1)} %bitcast.117), kind=kOutput, calls=%fused_computation.14 | convolution fusion | flops 1260748800 | bytes 5242880 | tf_op jit(solution)/shard_map/secd,df->secf/dot_general | solution.py:83
  157.8 2.2 fusion.2
  160.0 2.2 fusion.3
  162.2 0.7 pad_maximum_fusion
  163.0 3.4 %copy.32 = bf16[8,8,2,12,1280]{4,1,3,2,0:T(8,128)(2,1)} copy(bf16[8,8,2,12,1280]{4,3,1,0,2:T(8,128)(2,1)S(1)} %pad_maximum_fusion) | data formatting | bytes 7864320 | tf_op jit(solution)/shard_map/stack | solution.py:95
  166.4 51.6 %reduce-scatter.2.cloned.1.call-done = bf16[1,8,2,12,1280]{4,1,3,2,0:T(8,128)(2,1)} async-done(((bf16[8,8,2,12,1280]{4,1,3,2,0:T(8,128)(2,1)}), bf16[1,8,2,12,1280]{4,1,3,2,0:T(8,128)(2,1)}) %reduce-scatter.2.cloned.1.call-update) | async-done | bytes 491536 | tf_op jit(solution)/shard_map/reduce_scatter | solution.py:96
  218.0 1.5 copy.33
  219.5 16.5 %all_to_all.21 = bf16[8,2,12,1280]{3,1,2,0:T(2,128)(2,1)S(1)} all-to-all(bf16[8,2,12,1280]{3,1,2,0:T(2,128)(2,1)S(1)} %copy.33), channel_id=1, replica_groups=mesh['seq'=8,'exp'=8,'img'=4] {'exp'}, dimensions={0} | all-to-all | bytes 983040 | tf_op jit(solution)/shard_map/all_to_all | solution.py:97
  236.0 1.1 fusion.10
  (38 shorter events, 8.3 us)
Async XLA Ops:
  6.5 76.9 %all-gather.4.cloned.1.call-start = ((), (), s32[]{:S(2)}) async-start(), calls=%async_computation.5 | async-start | bytes 3686400 | tf_op jit(solution)/shard_map/all_gather | solution.py:58
  9.9 45.2 %all-to-all-start = ((bf16[3,8,160,128]{3,2,0,1:T(8,128)(2,1)}), bf16[3,8,160,128]{3,2,0,1:T(8,128)(2,1)S(1)}, u32[]{:S(2)}, u32[]{:S(2)}) async-start(bf16[3,8,160,128]{3,2,0,1:T(8,128)(2,1)} %copy.22), calls=%async_computation | async-start | bytes 1966080 | tf_op jit(solution)/shard_map/all_to_all | solution.py:49
  57.8 25.6 %copy-start = (bf16[1,128,1280]{2,1,0:T(8,128)(2,1)S(1)}, bf16[1,128,1280]{2,1,0:T(8,128)(2,1)}, u32[]{:S(2)}) copy-start(bf16[1,128,1280]{2,1,0:T(8,128)(2,1)} %param.9) | copy-start | bytes 983044
  62.2 24.1 %copy-start.1 = (f32[1280]{0:T(1024)S(1)}, f32[1280]{0:T(1024)}, u32[]{:S(2)}) copy-start(f32[1280]{0:T(1024)} %param.12) | copy-start | bytes 15364
  62.2 24.1 %copy-start.2 = (f32[1280]{0:T(1024)S(1)}, f32[1280]{0:T(1024)}, u32[]{:S(2)}) copy-start(f32[1280]{0:T(1024)} %param.11) | copy-start | bytes 15364
  64.7 18.7 %all-to-all-start.1 = ((bf16[8,1,128,1,160]{2,4,3,1,0:T(8,128)(2,1)}), bf16[8,1,128,1,160]{2,4,3,1,0:T(8,128)(2,1)S(1)}, u32[]{:S(2)}, u32[]{:S(2)}) async-start(bf16[8,1,128,1,160]{2,4,3,1,0:T(8,128)(2,1)} %constant_dynamic-update-slice_fusion), calls=%async_computation.1 | async-start | bytes 655360 | tf_op jit(solution)/shard_map/all_to_all | solution.py:53
  68.1 81.7 %all-gather.6.cloned.1.call-start = ((), (), s32[]{:S(2)}) async-start(), calls=%async_computation.7 | async-start | bytes 4423680 | tf_op jit(solution)/shard_map/all_gather | solution.py:80
  104.1 113.9 %reduce-scatter.2.cloned.1.call-start = ((), (), s32[]{:S(2)}) async-start(), calls=%async_computation.6 | async-start | bytes 4423680 | tf_op jit(solution)/shard_map/reduce_scatter | solution.py:96
  149.8 3.1 %copy-start.3 = (bf16[2,1280,640]{2,1,0:T(8,128)(2,1)S(1)}, bf16[2,1280,640]{2,1,0:T(8,128)(2,1)}, u32[]{:S(2)}) copy-start(bf16[2,1280,640]{2,1,0:T(8,128)(2,1)} %param.14) | copy-start | bytes 9830404
  155.4 2.5 %copy-start.4 = (bf16[2,640,1280]{2,1,0:T(8,128)(2,1)S(1)}, bf16[2,640,1280]{2,1,0:T(8,128)(2,1)}, u32[]{:S(2)}) copy-start(bf16[2,640,1280]{2,1,0:T(8,128)(2,1)} %param.15) | copy-start | bytes 9830404
Sparse Core Ops, SparseCore 0:
  9.1 68.4 all-gather.3
  104.2 45.5 all-gather.5
  166.5 51.4 reduce-scatter.1
